TPU v7x, 512 devices: a whole 4x4x16 slice. The times are simulated.
512 devices in a mesh: tensor: 4 (over x), request: 128 (over z, y, core).
Axes of the slice: x: 4, y: 4, z: 16, core: 2. Of those that a mesh axis runs over, the one named last changes fastest.
Arguments:
- hidden: bfloat16 [1024, 2048], P('request'), may hold values from -6 to 6
- norm_gain: float32 [2048], replicated, may hold values from 0.1 to 1.9
- w_query: bfloat16 [2048, 2048], P(None, 'tensor'), may hold values from -0.125 to 0.125
- w_keyval: bfloat16 [2048, 512], P(None, 'tensor'), may hold values from -0.125 to 0.125
- w_output: bfloat16 [2048, 2048], P('tensor'), may hold values from -0.125 to 0.125
- node_cache: bfloat16 [128, 4, 512, 128], P('request', 'tensor'), may hold values from -300 to 300
- leaf_cache: bfloat16 [1024, 4, 128, 128], P('request', 'tensor'), may hold values from -300 to 300
- leaf_branch: int32 [1024], replicated, may hold values from 0 to 63
- branch_root: int32 [64], replicated, may hold values from 0 to 7
- root_owner: int32 [8], replicated, may hold values from 0 to 127, as said below
- branch_owner: int32 [64], replicated, may hold values from 1 to 126, as said below
- root_len: int32 [8], replicated, may hold values from 1 to 512, as said below
- branch_len: int32 [64], replicated, may hold values from 1 to 512, as said below
- leaf_len: int32 [1024], P('request'), may hold values from 0 to 127, as said below
Outputs:
- mixed: bfloat16 [1024, 2048], P('request', 'tensor')
- new_entries: bfloat16 [1024, 4, 128], P('request', 'tensor')
Inputs may be any that keep to these rules, and one draw needn't show every extreme that they name: The 8 entries of root_owner are all different slots. `branch_owner`: different from every entry of root_owner and from one another. `root_len`: some root has exactly 512 positions. `branch_len`: some branch has exactly 512 positions. `leaf_len`: some leaf has exactly 127 positions.
All inputs are finite; a program needn't handle non-finite values.
Results may differ from a plain program's by a relative error of at most 0.029.
Values may be sent and summed in bfloat16 or wider, within the bound.
No kernel may reach another device: no remote copies, remote signals or barrier semaphores. Data moves between devices by JAX's collectives and lax.ppermute only.
A program may use at most 128 MiB of HBM per device.

v0:
```python
import jax
import jax.numpy as jnp
from jax import lax
from jax.sharding import PartitionSpec as P

FLOOR = -1e30


def rotate(values_in, positions):
    half_dim = values_in.shape[-1] // 2
    inverse_freq = 10000.0 ** (
        -(jnp.arange(half_dim, dtype=jnp.float32) * 2.0 / values_in.shape[-1])
    )
    angles = positions.astype(jnp.float32)[..., None] * inverse_freq
    angles = jnp.concatenate([angles, angles], -1)
    turned = jnp.concatenate([-values_in[..., half_dim:], values_in[..., :half_dim]], -1)
    return values_in * jnp.cos(angles) + turned * jnp.sin(angles)


def soft_part(scores, usable, value_rows, pattern):
    scores = jnp.where(usable, scores, FLOOR)
    peak = jnp.max(scores, -1)
    weights = jnp.where(usable, jnp.exp(scores - peak[..., None]), 0.0).astype(jnp.bfloat16)
    summed = jnp.einsum(pattern, weights, value_rows, preferred_element_type=jnp.float32)
    weight_sum = jnp.sum(weights.astype(jnp.float32), -1)
    return (summed, weight_sum, peak)


def local(
    hidden,
    norm_gain,
    w_query,
    w_keyval,
    w_output,
    node_cache,
    leaf_cache,
    leaf_branch,
    branch_root,
    root_owner,
    branch_owner,
    root_len,
    branch_len,
    leaf_len,
):
    head_dim = w_keyval.shape[1] // 2
    local_leaves = hidden.shape[0]
    group = w_query.shape[1] // head_dim
    factor = head_dim ** (-0.5)
    device = lax.axis_index("request")
    offset = device * local_leaves
    widened = hidden.astype(jnp.float32)
    normed = (
        widened * lax.rsqrt(jnp.mean(widened * widened, -1, keepdims=True) + 1e-05) * norm_gain
    ).astype(jnp.bfloat16)
    branch_ids = jnp.arange(branch_root.shape[0], dtype=jnp.int32)
    root_ids = jnp.arange(root_owner.shape[0], dtype=jnp.int32)
    branch_hits = leaf_branch[:, None] == branch_ids[None, :]
    leaf_root = jnp.sum(jnp.where(branch_hits, branch_root[None, :], 0), 1)
    root_hits = leaf_root[:, None] == root_ids[None, :]
    prefix_all = jnp.sum(jnp.where(root_hits, root_len[None, :], 0), 1) + jnp.sum(
        jnp.where(branch_hits, branch_len[None, :], 0), 1
    )
    positions = lax.dynamic_slice_in_dim(prefix_all, offset, local_leaves) + leaf_len
    raw_query = jnp.dot(normed, w_query, preferred_element_type=jnp.float32).reshape(
        local_leaves, group, head_dim
    )
    queries = rotate(raw_query, positions[:, None]).astype(jnp.bfloat16)
    raw_entry = jnp.dot(normed, w_keyval, preferred_element_type=jnp.float32)
    new_entry = jnp.concatenate(
        [rotate(raw_entry[:, :head_dim], positions), raw_entry[:, head_dim:]], -1
    ).astype(jnp.bfloat16)
    leaf_rows = leaf_cache[:, 0]
    slot_index = jnp.arange(leaf_rows.shape[1], dtype=jnp.int32)
    appended = jnp.where(
        (slot_index[None, :] == leaf_len[:, None])[:, :, None], new_entry[:, None, :], leaf_rows
    )
    leaf_scores = (
        jnp.einsum(
            "lgd,lkd->lgk", queries, appended[:, :, :head_dim], preferred_element_type=jnp.float32
        )
        * factor
    )
    leaf_usable = (slot_index[None, :] <= leaf_len[:, None])[:, None, :]
    leaf_sum, leaf_weight, leaf_peak = soft_part(
        leaf_scores, leaf_usable, appended[:, :, head_dim:], "lgk,lkd->lgd"
    )
    everyone = lax.all_gather(
        queries.reshape(local_leaves, group * head_dim), "request", axis=0, tiled=True
    )
    total_leaves = everyone.shape[0]
    mine_all = jnp.any(branch_hits & (branch_owner == device)[None, :], 1) | jnp.any(
        root_hits & (root_owner == device)[None, :], 1
    )
    my_length = jnp.sum(jnp.where(root_owner == device, root_len, 0)) + jnp.sum(
        jnp.where(branch_owner == device, branch_len, 0)
    )
    node_rows = node_cache[0, 0]
    node_usable = jnp.arange(node_rows.shape[0], dtype=jnp.int32) < my_length
    block_rows = 128
    block_count = total_leaves // block_rows

    def owner_block(stacked_in):
        rows_query, rows_mine = stacked_in
        scores = (
            jnp.einsum(
                "ngd,kd->ngk",
                rows_query,
                node_rows[:, :head_dim],
                preferred_element_type=jnp.float32,
            )
            * factor
        )
        usable = rows_mine[:, None, None] & node_usable[None, None, :]
        return soft_part(scores, usable, node_rows[:, head_dim:], "ngk,kd->ngd")

    results = lax.map(
        owner_block,
        (
            everyone.reshape(block_count, block_rows, group, head_dim),
            mine_all.reshape(block_count, block_rows),
        ),
    )
    own_sum = results[0].reshape(total_leaves, group, head_dim)
    own_weight = results[1].reshape(total_leaves, group)
    own_peak = results[2].reshape(total_leaves, group)
    global_peak = lax.pmax(own_peak.astype(jnp.bfloat16), "request").astype(own_peak.dtype)
    scaled = jnp.exp(own_peak - global_peak)
    shared_sum, remote_weight = (
        lax.psum_scatter(
            (scaled[..., None] * own_sum).reshape(total_leaves, group * head_dim),
            "request",
            scatter_dimension=0,
            tiled=True,
        ),
        lax.psum_scatter(scaled * own_weight, "request", scatter_dimension=0, tiled=True),
    )
    remote_sum = shared_sum.reshape(local_leaves, group, head_dim)
    remote_peak = lax.dynamic_slice_in_dim(global_peak, offset, local_leaves)
    peak = jnp.maximum(remote_peak, leaf_peak)
    remote_scale = jnp.exp(remote_peak - peak)
    leaf_scale = jnp.exp(leaf_peak - peak)
    numerator = remote_scale[..., None] * remote_sum + leaf_scale[..., None] * leaf_sum
    denominator = remote_scale * remote_weight + leaf_scale * leaf_weight
    attended = (
        (numerator / denominator[..., None])
        .astype(jnp.bfloat16)
        .reshape(local_leaves, group * head_dim)
    )
    term = jnp.dot(attended, w_output, preferred_element_type=jnp.float32)
    mixed = lax.psum_scatter(term, "tensor", scatter_dimension=1, tiled=True).astype(jnp.bfloat16)
    return (mixed, new_entry[:, None, :])


def solution(mesh):
    in_specs = (
        P("request", None),
        P(),
        P(None, "tensor"),
        P(None, "tensor"),
        P("tensor", None),
        P("request", "tensor", None, None),
        P("request", "tensor", None, None),
        P(),
        P(),
        P(),
        P(),
        P(),
        P(),
        P("request"),
    )
    out_specs = (P("request", "tensor"), P("request", "tensor", None))
    return jax.shard_map(local, mesh=mesh, in_specs=in_specs, out_specs=out_specs, check_vma=False)
```

profile of v0, /device:TPU:8, one launch (start us, length us, event | category | flops | bytes accessed | tf_op | source)
XLA Modules:
  0.0 1273.9 jit_solution(6114707259069529670)
XLA Ops:
  7.3 1.0 fusion.20
  8.4 1.3 fusion.27
  9.7 2.1 fusion.29
  16.9 132.0 %all-gather.2.cloned.1.call-done = bf16[1024,512]{1,0:T(8,128)(2,1)} async-done(((bf16[8,512]{1,0:T(8,128)(2,1)}), bf16[1024,512]{1,0:T(8,128)(2,1)}) %all-gather.2.cloned.1.call-update) | async-done | bytes 1048592 | tf_op jit(solution)/shard_map/all_gather | solution.py:87
  148.9 3.9 reshape.275
  152.8 2.3 copy.55
  155.1 88.6 %while.15 = (s32[]{:T(128)}, f32[8,128,8,64]{1,0,3,2:T(8,128)}, f32[8,128,8]{1,2,0:T(8,128)}, f32[8,128,8]{1,2,0:T(8,128)}, pred[8,128]{1,0:T(8,128)(4,1)}, /*in...) while((s32[]{:T(128)}, f32[8,128,8,64]{1,0,3,2:T(8,128)}, ...), condition=%wide.region_11.12_spmd.clone, body=%wide.region_8.11_spmd.clone.sunk | while | flops 142146048 | bytes 7636981 | solution.py:116
  157.8 0.7 fusion.52
  158.5 7.7 dynamic_update_slice.19
  168.8 0.7 fusion.52
  169.5 7.7 dynamic_update_slice.19
  179.9 0.7 fusion.52
  180.6 7.7 dynamic_update_slice.19
  191.7 7.7 dynamic_update_slice.19
  202.8 7.7 dynamic_update_slice.19
  213.1 0.7 fusion.52
  213.9 7.7 dynamic_update_slice.19
  224.2 0.7 fusion.52
  224.9 7.7 dynamic_update_slice.19
  236.0 7.7 dynamic_update_slice.19
  243.7 0.8 bitcast_convert_fusion
  244.5 489.9 %pmax.7 = bf16[1024,8]{0,1:T(8,128)(2,1)S(1)} all-reduce(bf16[1024,8]{0,1:T(8,128)(2,1)S(1)} %bitcast_convert_fusion), channel_id=1, replica_groups=mesh['tensor'=4,'request'=128] {'request'}, use_global_device_ids=true, to_apply=%region_12.13 | all-reduce | flops 8192 | bytes 32768 | tf_op jit(solution)/shard_map/pmax | solution.py:126
  734.4 0.8 bitcast_multiply_fusion.1
  735.2 3.4 bitcast_multiply_fusion
  738.6 2.9 copy.68
  741.7 0.8 copy-done.5
  743.6 1.3 dynamic-slice
  745.5 491.0 %all-reduce = f32[1024,8]{0,1:T(8,128)S(1)} all-reduce(f32[1024,8]{0,1:T(8,128)S(1)} %get-tuple-element.129), channel_id=3, replica_groups=mesh['tensor'=4,'request'=128] {'request'}, use_global_device_ids=true, to_apply=%region_15.16.clone | all-reduce | flops 8192 | bytes 65536
  1236.8 0.8 copy.69
  1238.1 1.0 fusion.42
  1239.9 26.2 %reduce-scatter.6.cloned.1.call-done = f32[8,512]{1,0:T(8,128)} async-done(((f32[8,2048]{1,0:T(8,128)}), f32[8,512]{1,0:T(8,128)}) %reduce-scatter.6.cloned.1.call-update) | async-done | bytes 16400 | tf_op jit(solution)/shard_map/reduce_scatter | solution.py:150
  1266.0 1.3 convert_element_type.60
  (128 shorter events, 29.7 us)
Async XLA Ops:
  7.2 1230.9 %copy-start = (bf16[512,2048]{1,0:T(8,128)(2,1)S(1)}, bf16[512,2048]{1,0:T(8,128)(2,1)}, u32[]{:S(2)}) copy-start(bf16[512,2048]{1,0:T(8,128)(2,1)} %param.20) | copy-start | bytes 6291460
  7.2 4.7 copy-start.7
  7.2 4.7 copy-start.13
  7.2 4.7 copy-start.10
  7.2 4.9 copy-start.8
  7.2 5.0 copy-start.9
  7.2 6.2 copy-start.6
  7.2 6.3 copy-start.11
  7.3 6.9 copy-start.12
  7.3 141.7 %all-gather.2.cloned.1.call-start = ((), (), s32[]{:S(2)}) async-start(), calls=%async_computation.2 | async-start | bytes 1056768 | tf_op jit(solution)/shard_map/all_gather | solution.py:87
  11.8 137.1 %copy-start.1 = (f32[8,8,64]{2,1,0:T(8,128)}, f32[8,8,64]{2,1,0:T(8,128)S(1)}, u32[]{:S(2)}) copy-start(f32[8,8,64]{2,1,0:T(8,128)S(1)} %reshape.266) | copy-start | bytes 49156
  12.5 136.4 %copy-start.3 = (f32[8,8,64]{2,1,0:T(8,128)}, f32[8,8,64]{2,1,0:T(8,128)S(1)}, u32[]{:S(2)}) copy-start(f32[8,8,64]{2,1,0:T(8,128)S(1)} %maximum_multiply_fusion) | copy-start | bytes 49156
  13.3 1223.4 %reduce-scatter.8.cloned.1.call-start = ((), (), s32[]{:S(2)}) async-start(), calls=%async_computation.4 | async-start | bytes 2113536
  741.5 0.9 copy-start.5
  741.5 1.5 copy-start.2
  741.5 1.5 copy-start.4
  741.5 524.5 %reduce-scatter.6.cloned.1.call-start = ((), (), s32[]{:S(2)}) async-start(), calls=%async_computation.3 | async-start | bytes 81920 | tf_op jit(solution)/shard_map/reduce_scatter | solution.py:150
Sparse Core Ops, SparseCore 0:
  13.5 135.4 all-gather.1
  741.7 260.9 reduce-scatter.7
  1239.3 26.7 reduce-scatter.5
where the time goes:
time: 1280 us; the launch traced here: 1270 us
  blocking collectives  981 us (77%)
  waiting for transfers between devices  158 us (12%)
  local copies, waits for them, and re-layouts  85.3 us (7%)
  other arithmetic  18.2 us (1%)
  between operations  15.9 us (1%)
  matrix products  15 us (1%)
    unnamed x1, blocking collectives  491 us
    pmax x1, blocking collectives, local(): lax.pmax(own_peak.astype(jnp.bfloat16), 'request').astype(own_peak.dtype)  490 us
    all_gather x1, waiting for transfers between devices, local(): lax.all_gather(queries.reshape(local_leaves, group * head_dim), 'request'...  132 us
    dynamic_update_slice x16, local copies, waits for them, and re-layouts, local(): lax.map(owner_block, (everyone.reshape(block_count, block_rows, group, he...  66.5 us
    reduce_scatter x1, waiting for transfers between devices, local(): lax.psum_scatter(term, 'tensor', scatter_dimension=1, tiled=True)  26.2 us
  transfers between devices with their start and end apart: 3, of which 2 were waited for; matrix products, arithmetic and copies ran while one was open for 0% of the time, Pallas kernels for 0%

commit v1 on v0

--- a/solution.py
+++ b/solution.py
@@ -84,8 +84,14 @@
     leaf_sum, leaf_weight, leaf_peak = soft_part(
         leaf_scores, leaf_usable, appended[:, :, head_dim:], "lgk,lkd->lgd"
     )
-    everyone = lax.all_gather(
-        queries.reshape(local_leaves, group * head_dim), "request", axis=0, tiled=True
+    everyone = jnp.concatenate(
+        lax.all_to_all(
+            jnp.stack([queries.reshape(local_leaves, group * head_dim)] * lax.axis_size("request")),
+            "request",
+            0,
+            0,
+        ),
+        axis=0,
     )
     total_leaves = everyone.shape[0]
     mine_all = jnp.any(branch_hits & (branch_owner == device)[None, :], 1) | jnp.any(

time: 1280 us -> 1210 us (0.945)
  waiting for transfers between devices: 158 us -> 76.9 us
  starting transfers between devices: 0.12 us -> 19.6 us
    all_gather x1 -> x0, waiting for transfers between devices: 132 us -> none  [local(): lax.all_gather(queries.reshape(local_leaves, group * head_dim), 'request'...]
    all_to_all x0 -> x1, waiting for transfers between devices: none -> 49.1 us  [local(): lax.all_to_all(jnp.stack([queries.reshape(local_leaves, group * head_dim)...]
    all_to_all x0 -> x1, starting transfers between devices: none -> 19.5 us  [local(): lax.all_to_all(jnp.stack([queries.reshape(local_leaves, group * head_dim)...]
where the time goes in v1:
time: 1210 us
  blocking collectives  978 us (81%)
  local copies, waits for them, and re-layouts  84.5 us (7%)
  waiting for transfers between devices  76.9 us (6%)
  starting transfers between devices  19.6 us (2%)
  other arithmetic  17.5 us (1%)
  between operations  16.1 us (1%)
  matrix products  15 us (1%)
    unnamed x1, blocking collectives  491 us
    pmax x1, blocking collectives, local(): lax.pmax(own_peak.astype(jnp.bfloat16), 'request').astype(own_peak.dtype)  487 us
    dynamic_update_slice x16, local copies, waits for them, and re-layouts, local(): lax.map(owner_block, (everyone.reshape(block_count, block_rows, group, he...  66.5 us
    all_to_all x1, waiting for transfers between devices, local(): lax.all_to_all(jnp.stack([queries.reshape(local_leaves, group * head_dim)...  49.1 us
    reduce_scatter x1, waiting for transfers between devices, local(): lax.psum_scatter(term, 'tensor', scatter_dimension=1, tiled=True)  27.7 us
  transfers between devices with their start and end apart: 3, of which 2 were waited for; matrix products, arithmetic and copies ran while one was open for 0% of the time, Pallas kernels for 0%

profile of v1, /device:TPU:8, one launch (start us, length us, event | category | flops | bytes accessed | tf_op | source)
XLA Modules:
  0.0 1207.9 jit_solution(12266339730740072560)
XLA Ops:
  7.3 1.0 fusion.20
  8.3 1.3 fusion.27
  9.6 2.1 fusion.29
  12.6 1.1 stack.3
  13.7 19.5 %all-to-all-start = ((bf16[128,8,512]{2,1,0:T(8,128)(2,1)}), bf16[128,8,512]{2,1,0:T(8,128)(2,1)S(1)}, u32[]{:S(2)}, u32[]{:S(2)}) async-start(bf16[128,8,512]{2,1,0:T(8,128)(2,1)} %stack.3), calls=%async_computation | async-start | bytes 2097152 | tf_op jit(solution)/shard_map/all_to_all | solution.py:88
  36.6 49.1 %all-to-all-done = bf16[128,8,512]{2,1,0:T(8,128)(2,1)S(1)} async-done(((bf16[128,8,512]{2,1,0:T(8,128)(2,1)}), bf16[128,8,512]{2,1,0:T(8,128)(2,1)S(1)}, u32[]{:S(2)}, u32[]{:S(2)}) %all-to-all-start) | async-done | bytes 1048608 | tf_op jit(solution)/shard_map/all_to_all | solution.py:88
  85.8 2.1 reshape_reshape.3
  87.8 2.3 copy.50
  90.1 88.6 %while.15 = (s32[]{:T(128)}, f32[8,128,8,64]{1,0,3,2:T(8,128)}, f32[8,128,8]{1,2,0:T(8,128)}, f32[8,128,8]{1,2,0:T(8,128)}, pred[8,128]{1,0:T(8,128)(4,1)}, /*in...) while((s32[]{:T(128)}, f32[8,128,8,64]{1,0,3,2:T(8,128)}, ...), condition=%wide.region_11.12_spmd.clone, body=%wide.region_8.11_spmd.clone.sunk | while | flops 142146048 | bytes 7636981 | solution.py:122
  93.5 7.7 dynamic_update_slice.19
  104.5 7.7 dynamic_update_slice.19
  115.6 7.7 dynamic_update_slice.19
  126.7 7.7 dynamic_update_slice.19
  137.0 0.7 fusion.52
  137.8 7.7 dynamic_update_slice.19
  148.8 7.7 dynamic_update_slice.19
  159.2 0.7 fusion.52
  159.9 7.7 dynamic_update_slice.19
  170.3 0.7 fusion.52
  171.0 7.7 dynamic_update_slice.19
  178.7 0.8 bitcast_convert_fusion
  179.4 487.1 %pmax.7 = bf16[1024,8]{0,1:T(8,128)(2,1)S(1)} all-reduce(bf16[1024,8]{0,1:T(8,128)(2,1)S(1)} %bitcast_convert_fusion), channel_id=1, replica_groups=mesh['tensor'=4,'request'=128] {'request'}, use_global_device_ids=true, to_apply=%region_12.13 | all-reduce | flops 8192 | bytes 32768 | tf_op jit(solution)/shard_map/pmax | solution.py:132
  666.6 0.8 bitcast_multiply_fusion.1
  667.4 3.4 bitcast_multiply_fusion
  670.7 2.9 copy.61
  673.8 0.8 copy-done.5
  675.7 1.3 dynamic-slice
  677.7 491.0 %all-reduce = f32[1024,8]{0,1:T(8,128)S(1)} all-reduce(f32[1024,8]{0,1:T(8,128)S(1)} %get-tuple-element.121), channel_id=3, replica_groups=mesh['tensor'=4,'request'=128] {'request'}, use_global_device_ids=true, to_apply=%region_15.16.clone | all-reduce | flops 8192 | bytes 65536
  1169.0 0.8 copy.62
  1170.3 1.0 fusion.42
  1172.1 27.7 %reduce-scatter.6.cloned.1.call-done = f32[8,512]{1,0:T(8,128)} async-done(((f32[8,2048]{1,0:T(8,128)}), f32[8,512]{1,0:T(8,128)}) %reduce-scatter.6.cloned.1.call-update) | async-done | bytes 16400 | tf_op jit(solution)/shard_map/reduce_scatter | solution.py:156
  1199.8 1.3 convert_element_type.61
  (128 shorter events, 30.4 us)
Async XLA Ops:
  7.2 1163.1 %copy-start = (bf16[512,2048]{1,0:T(8,128)(2,1)S(1)}, bf16[512,2048]{1,0:T(8,128)(2,1)}, u32[]{:S(2)}) copy-start(bf16[512,2048]{1,0:T(8,128)(2,1)} %param.20) | copy-start | bytes 6291460
  7.2 4.6 copy-start.7
  7.2 4.6 copy-start.13
  7.2 4.6 copy-start.10
  7.2 4.8 copy-start.8
  7.2 4.9 copy-start.9
  11.6 21.6 %copy-start.6 = (bf16[1,1,512,128]{3,2,1,0:T(8,128)(2,1)S(1)}, bf16[1,1,512,128]{3,2,1,0:T(8,128)(2,1)}, u32[]{:S(2)}) copy-start(bf16[1,1,512,128]{3,2,1,0:T(8,128)(2,1)} %param.21) | copy-start | bytes 393220
  11.7 21.8 %copy-start.11 = (s32[8]{0:T(128)S(1)}, s32[8]{0:T(128)}, u32[]{:S(2)}) copy-start(s32[8]{0:T(128)} %param.25) | copy-start | bytes 100
  11.7 22.4 %copy-start.12 = (s32[64]{0:T(128)S(1)}, s32[64]{0:T(128)}, u32[]{:S(2)}) copy-start(s32[64]{0:T(128)} %param.26) | copy-start | bytes 772
  11.7 1.9 copy-start.1
  12.4 1.2 copy-start.3
  13.7 72.1 %all-to-all-start = ((bf16[128,8,512]{2,1,0:T(8,128)(2,1)}), bf16[128,8,512]{2,1,0:T(8,128)(2,1)S(1)}, u32[]{:S(2)}, u32[]{:S(2)}) async-start(bf16[128,8,512]{2,1,0:T(8,128)(2,1)} %stack.3), calls=%async_computation | async-start | bytes 2097152 | tf_op jit(solution)/shard_map/all_to_all | solution.py:88
  33.2 1135.8 %reduce-scatter.8.cloned.1.call-start = ((), (), s32[]{:S(2)}) async-start(), calls=%async_computation.4 | async-start | bytes 2113536
  673.7 0.9 copy-start.5
  673.7 1.5 copy-start.2
  673.7 1.5 copy-start.4
  673.7 526.1 %reduce-scatter.6.cloned.1.call-start = ((), (), s32[]{:S(2)}) async-start(), calls=%async_computation.3 | async-start | bytes 81920 | tf_op jit(solution)/shard_map/reduce_scatter | solution.py:156
Sparse Core Ops, SparseCore 0:
  673.8 262.5 reduce-scatter.7
  1171.5 28.2 reduce-scatter.5
